TPU v7x, 512 devices: a whole 4x4x16 slice. The times are simulated.
512 devices in a mesh: seq: 64 (over z, x_hi, core), section: 8 (over y, x_lo).
Axes of the slice: x: 4 (x_hi: 2, x_lo: 2; x = x_hi * 2 + x_lo), y: 4, z: 16, core: 2. Of those that a mesh axis runs over, the one named last changes fastest.
Arguments:
- fwd_input: bfloat16 [8, 16384, 768], P('section', 'seq'), may hold values from -6 to 6
- bwd_input: bfloat16 [8, 16384, 768], P('section', 'seq'), may hold values from -6 to 6
- bwd_cotangent: bfloat16 [8, 16384, 768], P('section', 'seq'), may hold values from -6 to 6
- conv_weight: bfloat16 [8, 2, 3, 768, 384], P('section', None, None, 'seq'), may hold values from -0.125 to 0.125
- proj_weight: bfloat16 [8, 2, 384, 768], P('section', None, 'seq'), may hold values from -0.3125 to 0.3125
Outputs:
- next_input: bfloat16 [8, 16384, 768], P('section', 'seq')
- prev_cotangent: bfloat16 [8, 16384, 768], P('section', 'seq')
All inputs are finite; a program needn't handle non-finite values.
Results may differ from a plain program's by a relative error of at most 0.012.
Values may be sent and summed in bfloat16 or wider, within the bound.
No kernel may reach another device: no remote copies, remote signals or barrier semaphores. Data moves between devices by JAX's collectives and lax.ppermute only.
A program may use at most 64 MiB of HBM per device.

v0:
```python
import jax
import jax.numpy as jnp
from jax import lax
from jax.sharding import PartitionSpec as P

BLOCKS = 2
FIRST_DILATION = 128


def padded(x, sides, width):
    for axis, dim in sides:
        size, length = (lax.axis_size(axis), x.shape[dim])
        up = [(i, (i + 1) % size) for i in range(size - 1)]
        down = [(j, i) for i, j in up]
        last = lax.slice_in_dim(x, length - width, length, axis=dim)
        initial = lax.slice_in_dim(x, 0, width, axis=dim)
        before = lax.ppermute(last, axis, up)
        after = lax.ppermute(initial, axis, down)
        x = jnp.concatenate([before, x, after], axis=dim)
    return x


def from_behind(block, axis, distance):
    devices = range(lax.axis_size(axis))
    route = [(i - distance, i) for i in devices if i - distance in devices]
    return lax.ppermute(block, axis, route)


def from_behind_2(block, axis, distance):
    devices = range(lax.axis_size(axis))
    route = [((i - distance) % len(devices), i) for i in devices]
    return lax.ppermute(block, axis, route)


def gelu_back(value, cotangent):
    return jax.vjp(jax.nn.gelu, value)[1](cotangent)[0]


def rounded(product):
    return lax.optimization_barrier(product.astype(jnp.bfloat16)).astype(jnp.float32)


def reach(values, spacing_gap):
    length = values.shape[1]
    if spacing_gap < length:
        padded_input = padded(values, (("seq", 1),), spacing_gap)
        return (padded_input[:, :length], padded_input[:, 2 * spacing_gap :])
    shard_hops = spacing_gap // length
    earlier = from_behind(values, "seq", shard_hops)
    later = from_behind(values, "seq", -shard_hops)
    return (earlier, later)


def conv_apply(values, weight):
    return jnp.einsum("krc,ch->krh", values, weight, preferred_element_type=jnp.float32)


def conv_transpose(values, weight):
    return jnp.einsum("krh,ch->krc", values, weight, preferred_element_type=jnp.float32)


def run_forward(present_state, pieces):
    stored = []
    for depth_level in range(BLOCKS):
        conv_part, proj_part = pieces[depth_level]
        spacing_gap = FIRST_DILATION * 4**depth_level
        activated = jax.nn.gelu(present_state.astype(jnp.float32)).astype(jnp.bfloat16)
        middle = conv_apply(activated, conv_part[1])
        earlier, later = reach(activated, spacing_gap)
        preact = (
            rounded(conv_apply(earlier, conv_part[0]))
            + middle
            + rounded(conv_apply(later, conv_part[2]))
        )
        hidden = jax.nn.gelu(preact).astype(jnp.bfloat16)
        stored.append((present_state, preact))
        branch = jnp.einsum("krh,hc->krc", hidden, proj_part, preferred_element_type=jnp.float32)
        present_state = (present_state.astype(jnp.float32) + branch).astype(jnp.bfloat16)
    return (present_state, stored)


def local(fwd_input, bwd_input, bwd_cotangent, conv_weight, proj_weight):
    convolution_complete, proj_full = (
        lax.all_gather(conv_weight, "seq", axis=3, tiled=True),
        lax.all_gather(proj_weight, "seq", axis=2, tiled=True),
    )
    pieces = [
        (convolution_complete[0, depth_level], proj_full[0, depth_level])
        for depth_level in range(BLOCKS)
    ]
    forward_out, unused = run_forward(fwd_input, pieces)
    unused_out, stored = run_forward(bwd_input, pieces)
    cotangent = bwd_cotangent
    for depth_level in reversed(range(BLOCKS)):
        conv_part, proj_part = pieces[depth_level]
        spacing_gap = FIRST_DILATION * 4**depth_level
        block_in, preact = stored[depth_level]
        d_hidden = jnp.einsum(
            "krc,hc->krh", cotangent, proj_part, preferred_element_type=jnp.float32
        )
        d_preact = gelu_back(preact, d_hidden).astype(jnp.bfloat16)
        earlier, later = reach(d_preact, spacing_gap)
        d_act = (
            conv_transpose(later, conv_part[0])
            + conv_transpose(d_preact, conv_part[1])
            + conv_transpose(earlier, conv_part[2])
        )
        total = cotangent.astype(jnp.float32) + gelu_back(block_in.astype(jnp.float32), d_act)
        cotangent = total.astype(jnp.bfloat16)
    next_input = from_behind_2(forward_out, "section", 1)
    prev_cotangent = from_behind_2(cotangent, "section", -1)
    return (next_input, prev_cotangent)


def solution(mesh):
    in_specs = (
        P("section", "seq", None),
        P("section", "seq", None),
        P("section", "seq", None),
        P("section", None, None, "seq", None),
        P("section", None, "seq", None),
    )
    out_specs = (P("section", "seq", None), P("section", "seq", None))
    return jax.shard_map(local, mesh=mesh, in_specs=in_specs, out_specs=out_specs, check_vma=False)
```

profile of v0, /device:TPU:103, one launch (start us, length us, event | category | flops | bytes accessed | tf_op | source)
XLA Modules:
  0.0 411.6 jit_solution(7806383991603172441)
XLA Ops:
  8.0 1.5 copy.9
  11.6 6.1 %collective-permute-start.5 = (bf16[1,128,768]{2,1,0:T(8,128)(2,1)}, bf16[1,128,768]{2,1,0:T(8,128)(2,1)}, u32[]{:S(2)}, u32[]{:S(2)}) collective-permute-start(bf16[1,128,768]{2,1,0:T(8,128)(2,1)} %get-tuple-element.10), channel_id=1, source_target_pairs={{0,8},{8,16},{16,24},{24,32},{32,40},{40,48},{48,56},{56,64},{64,7... | collective-permute-start | bytes 589832 | tf_op jit(solution)/shard_map/ppermute | solution.py:17
  17.7 1.9 collective-permute-start.6
  21.5 7.2 %collective-permute-start = (bf16[1,128,768]{2,1,0:T(8,128)(2,1)}, bf16[1,128,768]{2,1,0:T(8,128)(2,1)}, u32[]{:S(2)}, u32[]{:S(2)}) collective-permute-start(bf16[1,128,768]{2,1,0:T(8,128)(2,1)} %get-tuple-element.12), channel_id=1, source_target_pairs={{0,8},{8,16},{16,24},{24,32},{32,40},{40,48},{48,56},{56,64},{64,7... | collective-permute-start | bytes 589832 | tf_op jit(solution)/shard_map/ppermute | solution.py:17
  28.8 1.9 collective-permute-start.1
  30.7 123.7 %all-gather.5.cloned.1.call-done = bf16[1,2,384,768]{3,1,0,2:T(2,128)(2,1)} async-done(((bf16[1,2,6,768]{3,1,0,2:T(2,128)(2,1)}), bf16[1,2,384,768]{3,1,0,2:T(2,128)(2,1)}) %all-gather.5.cloned.1.call-update) | async-done | bytes 1179664 | tf_op jit(solution)/shard_map/all_gather | solution.py:85
  154.4 5.1 %fusion.172 = (bf16[1,1,384,768]{3,1,0,2:T(2,128)(2,1)}, bf16[1,1,384,768]{3,1,0,2:T(2,128)(2,1)}) fusion(bf16[1,2,384,768]{3,1,0,2:T(2,128)(2,1)} %all-gather.5.cloned.1.call-done), kind=kLoop, calls=%fused_computation.215 | loop fusion | bytes 2359296 | tf_op jit(solution)/shard_map/slice | solution.py:88
  159.5 141.4 %all-gather.3.cloned.1.call-done = bf16[1,2,3,768,384]{4,1,2,0,3:T(2,128)(2,1)} async-done(((bf16[1,2,3,12,384]{4,1,2,0,3:T(2,128)(2,1)}), bf16[1,2,3,768,384]{4,1,2,0,3:T(2,128)(2,1)}) %all-gather.3.cloned.1.call-update) | async-done | bytes 3538960 | tf_op jit(solution)/shard_map/all_gather | solution.py:84
  300.9 9.0 %fusion.171 = (bf16[1,1,1,768,384]{4,1,2,0,3:T(2,128)(2,1)}, bf16[1,1,1,768,384]{4,1,2,0,3:T(2,128)(2,1)}, bf16[1,1,1,768,384]{4,1,2,0,3:T(2,128)(2,1)S(1)}, bf1...) fusion(bf16[1,2,3,768,384]{4,1,2,0,3:T(2,128)(2,1)} %all-gather, ...), kind=kLoop, calls=%fused_computation.214 | loop fusion | bytes 7077888 | tf_op jit(solution)/shard_map/slice | solution.py:68
  310.0 1.5 fusion.19
  314.2 1.4 fusion.48
  315.6 3.8 collective-permute-start.7
  319.4 3.0 collective-permute-start.8
  322.4 2.0 fusion.15
  324.4 2.0 fusion.16
  326.4 3.5 fusion.44
  329.9 5.9 %collective-permute-start.2 = (bf16[1,256,768]{2,1,0:T(8,128)(2,1)}, bf16[1,256,768]{2,1,0:T(8,128)(2,1)S(1)}, u32[]{:S(2)}, u32[]{:S(2)}) collective-permute-start(bf16[1,256,768]{2,1,0:T(8,128)(2,1)} %get-tuple-element.16), channel_id=1, source_target_pairs={{0,16},{8,24},{16,32},{24,40},{32,48},{40,56},{48,64},{56,72},{64,... | collective-permute-start | bytes 1179656 | tf_op jit(solution)/shard_map/ppermute | solution.py:26
  335.8 1.9 collective-permute-start.3
  338.1 1.9 fusion.21
  340.0 6.2 %collective-permute-done.8 = bf16[1,256,768]{2,1,0:T(8,128)(2,1)} collective-permute-done((bf16[1,256,768]{2,1,0:T(8,128)(2,1)}, bf16[1,256,768]{2,1,0:T(8,128)(2,1)}, u32[]{:S(2)}, u32[]{:S(2)}) %collective-permute-start.8) | collective-permute-done | bytes 393248 | tf_op jit(solution)/shard_map/ppermute | solution.py:26
  350.1 6.9 %collective-permute-start.10 = (bf16[1,256,384]{2,1,0:T(8,128)(2,1)}, bf16[1,256,384]{2,1,0:T(8,128)(2,1)}, u32[]{:S(2)}, u32[]{:S(2)}) collective-permute-start(bf16[1,256,384]{2,1,0:T(8,128)(2,1)} %fusion.70), channel_id=1, source_target_pairs={{0,16},{8,24},{16,32},{24,40},{32,48},{40,56},{48,64},{56,72},{64,... | collective-permute-start | bytes 589832 | tf_op jit(solution)/shard_map/ppermute | solution.py:26
  357.0 2.1 collective-permute-start.9
  361.3 3.5 fusion.5
  364.8 3.4 collective-permute-start.4
  368.2 1.8 fusion.132
  370.1 1.4 fusion.130
  371.6 1.9 fusion.32
  374.0 8.8 %collective-permute-start.12 = (bf16[1,128,384]{2,1,0:T(8,128)(2,1)S(1)}, bf16[1,128,384]{2,1,0:T(8,128)(2,1)S(1)}, u32[]{:S(2)}, u32[]{:S(2)}) collective-permute-start(bf16[1,128,384]{2,1,0:T(8,128)(2,1)S(1)} %get-tuple-element.15), channel_id=1, source_target_pairs={{0,8},{8,16},{16,24},{24,32},{32,40},{40,48},{48,56},{56,64},{64,7... | collective-permute-start | bytes 294920 | tf_op jit(solution)/shard_map/ppermute | solution.py:17
  383.3 2.1 collective-permute-start.11
  385.7 7.3 %collective-permute-done.11 = bf16[1,128,384]{2,1,0:T(8,128)(2,1)S(1)} collective-permute-done((bf16[1,128,384]{2,1,0:T(8,128)(2,1)S(1)}, bf16[1,128,384]{2,1,0:T(8,128)(2,1)S(1)}, u32[]{:S(2)}, u32[]{:S(2)}) %collective-permute-start.11) | collective-permute-done | bytes 98336 | tf_op jit(solution)/shard_map/ppermute | solution.py:18
  393.9 1.9 collective-permute-start.13
  395.8 7.5 %collective-permute-done.13 = bf16[1,256,768]{2,1,0:T(8,128)(2,1)S(1)} collective-permute-done((bf16[1,256,768]{2,1,0:T(8,128)(2,1)S(1)}, bf16[1,256,768]{2,1,0:T(8,128)(2,1)S(1)}, u32[]{:S(2)}, u32[]{:S(2)}) %collective-permute-start.13) | collective-permute-done | bytes 393248 | tf_op jit(solution)/shard_map/ppermute | solution.py:32
  (75 shorter events, 17.4 us)
Async XLA Ops:
  7.2 12.5 %copy-start.12 = (bf16[1,256,768]{2,1,0:T(8,128)(2,1)S(1)}, bf16[1,256,768]{2,1,0:T(8,128)(2,1)}, u32[]{:S(2)}) copy-start(bf16[1,256,768]{2,1,0:T(8,128)(2,1)} %param.5) | copy-start | bytes 1179652
  7.2 147.3 %all-gather.5.cloned.1.call-start = ((), (), s32[]{:S(2)}) async-start(), calls=%async_computation.1 | async-start | bytes 1198080 | tf_op jit(solution)/shard_map/all_gather | solution.py:85
  7.9 293.0 %all-gather.3.cloned.1.call-start = ((), (), s32[]{:S(2)}) async-start(), calls=%async_computation | async-start | bytes 3594240 | tf_op jit(solution)/shard_map/all_gather | solution.py:84
  10.7 7.0 %copy-start.3 = (bf16[1,256,768]{2,1,0:T(8,128)(2,1)}, bf16[1,256,768]{2,1,0:T(8,128)(2,1)S(1)}, u32[]{:S(2)}) copy-start(bf16[1,256,768]{2,1,0:T(8,128)(2,1)S(1)} %fusion.54) | copy-start | bytes 1179652
  11.6 298.4 %collective-permute-start.5 = (bf16[1,128,768]{2,1,0:T(8,128)(2,1)}, bf16[1,128,768]{2,1,0:T(8,128)(2,1)}, u32[]{:S(2)}, u32[]{:S(2)}) collective-permute-start(bf16[1,128,768]{2,1,0:T(8,128)(2,1)} %get-tuple-element.10), channel_id=1, source_target_pairs={{0,8},{8,16},{16,24},{24,32},{32,40},{40,48},{48,56},{56,64},{64,7... | collective-permute-start | bytes 589832 | tf_op jit(solution)/shard_map/ppermute | solution.py:17
  17.7 293.8 %collective-permute-start.6 = (bf16[1,128,768]{2,1,0:T(8,128)(2,1)}, bf16[1,128,768]{2,1,0:T(8,128)(2,1)}, u32[]{:S(2)}, u32[]{:S(2)}) collective-permute-start(bf16[1,128,768]{2,1,0:T(8,128)(2,1)} %get-tuple-element.11), channel_id=1, source_target_pairs={{8,0},{16,8},{24,16},{32,24},{40,32},{48,40},{56,48},{64,56},{72,6... | collective-permute-start | bytes 589832 | tf_op jit(solution)/shard_map/ppermute | solution.py:18
  21.5 300.9 %collective-permute-start = (bf16[1,128,768]{2,1,0:T(8,128)(2,1)}, bf16[1,128,768]{2,1,0:T(8,128)(2,1)}, u32[]{:S(2)}, u32[]{:S(2)}) collective-permute-start(bf16[1,128,768]{2,1,0:T(8,128)(2,1)} %get-tuple-element.12), channel_id=1, source_target_pairs={{0,8},{8,16},{16,24},{24,32},{32,40},{40,48},{48,56},{56,64},{64,7... | collective-permute-start | bytes 589832 | tf_op jit(solution)/shard_map/ppermute | solution.py:17
  28.8 295.7 %collective-permute-start.1 = (bf16[1,128,768]{2,1,0:T(8,128)(2,1)}, bf16[1,128,768]{2,1,0:T(8,128)(2,1)}, u32[]{:S(2)}, u32[]{:S(2)}) collective-permute-start(bf16[1,128,768]{2,1,0:T(8,128)(2,1)} %get-tuple-element.13), channel_id=1, source_target_pairs={{8,0},{16,8},{24,16},{32,24},{40,32},{48,40},{56,48},{64,56},{72,6... | collective-permute-start | bytes 589832 | tf_op jit(solution)/shard_map/ppermute | solution.py:18
  300.9 9.0 %copy-start.4 = (bf16[1,256,768]{2,1,0:T(8,128)(2,1)S(1)}, bf16[1,256,768]{2,1,0:T(8,128)(2,1)}, u32[]{:S(2)}) copy-start(bf16[1,256,768]{2,1,0:T(8,128)(2,1)} %copy-done.3) | copy-start | bytes 1179652
  310.0 12.5 %copy-start.5 = (bf16[1,1,1,768,384]{4,1,2,0,3:T(2,128)(2,1)}, bf16[1,1,1,768,384]{4,1,2,0,3:T(2,128)(2,1)S(1)}, u32[]{:S(2)}) copy-start(bf16[1,1,1,768,384]{4,1,2,0,3:T(2,128)(2,1)S(1)} %get-tuple-element.6) | copy-start | bytes 1769476
  313.4 2.2 copy-start.17
  314.2 8.3 %copy-start.2 = (bf16[1,256,768]{2,1,0:T(8,128)(2,1)S(1)}, bf16[1,256,768]{2,1,0:T(8,128)(2,1)}, u32[]{:S(2)}) copy-start(bf16[1,256,768]{2,1,0:T(8,128)(2,1)} %copy-done.1) | copy-start | bytes 1179652
  315.6 22.5 %collective-permute-start.7 = (bf16[1,256,768]{2,1,0:T(8,128)(2,1)}, bf16[1,256,768]{2,1,0:T(8,128)(2,1)}, u32[]{:S(2)}, u32[]{:S(2)}) collective-permute-start(bf16[1,256,768]{2,1,0:T(8,128)(2,1)} %get-tuple-element.18), channel_id=1, source_target_pairs={{0,16},{8,24},{16,32},{24,40},{32,48},{40,56},{48,64},{56,72},{64,... | collective-permute-start | bytes 1179656 | tf_op jit(solution)/shard_map/ppermute | solution.py:26
  319.4 26.8 %collective-permute-start.8 = (bf16[1,256,768]{2,1,0:T(8,128)(2,1)}, bf16[1,256,768]{2,1,0:T(8,128)(2,1)}, u32[]{:S(2)}, u32[]{:S(2)}) collective-permute-start(bf16[1,256,768]{2,1,0:T(8,128)(2,1)} %get-tuple-element.18), channel_id=1, source_target_pairs={{16,0},{24,8},{32,16},{40,24},{48,32},{56,40},{64,48},{72,56},{80,... | collective-permute-start | bytes 1179656 | tf_op jit(solution)/shard_map/ppermute | solution.py:26
  329.9 29.2 %collective-permute-start.2 = (bf16[1,256,768]{2,1,0:T(8,128)(2,1)}, bf16[1,256,768]{2,1,0:T(8,128)(2,1)S(1)}, u32[]{:S(2)}, u32[]{:S(2)}) collective-permute-start(bf16[1,256,768]{2,1,0:T(8,128)(2,1)} %get-tuple-element.16), channel_id=1, source_target_pairs={{0,16},{8,24},{16,32},{24,40},{32,48},{40,56},{48,64},{56,72},{64,... | collective-permute-start | bytes 1179656 | tf_op jit(solution)/shard_map/ppermute | solution.py:26
  335.8 24.4 %collective-permute-start.3 = (bf16[1,256,768]{2,1,0:T(8,128)(2,1)}, bf16[1,256,768]{2,1,0:T(8,128)(2,1)S(1)}, u32[]{:S(2)}, u32[]{:S(2)}) collective-permute-start(bf16[1,256,768]{2,1,0:T(8,128)(2,1)} %get-tuple-element.16), channel_id=1, source_target_pairs={{16,0},{24,8},{32,16},{40,24},{48,32},{56,40},{64,48},{72,56},{80,... | collective-permute-start | bytes 1179656 | tf_op jit(solution)/shard_map/ppermute | solution.py:26
  338.1 9.4 %copy-start = (bf16[1,1,1,768,384]{4,1,2,0,3:T(2,128)(2,1)S(1)}, bf16[1,1,1,768,384]{4,1,2,0,3:T(2,128)(2,1)}, u32[]{:S(2)}) copy-start(bf16[1,1,1,768,384]{4,1,2,0,3:T(2,128)(2,1)} %get-tuple-element.2) | copy-start | bytes 1769476
  338.1 9.4 %copy-start.19 = (bf16[1,256,768]{2,1,0:T(8,128)(2,1)S(1)}, bf16[1,256,768]{2,1,0:T(8,128)(2,1)}, u32[]{:S(2)}) copy-start(bf16[1,256,768]{2,1,0:T(8,128)(2,1)} %get-tuple-element.19) | copy-start | bytes 1179652
  348.9 10.2 %copy-start.7 = (bf16[1,1,1,768,384]{4,1,2,0,3:T(2,128)(2,1)S(1)}, bf16[1,1,1,768,384]{4,1,2,0,3:T(2,128)(2,1)}, u32[]{:S(2)}) copy-start(bf16[1,1,1,768,384]{4,1,2,0,3:T(2,128)(2,1)} %get-tuple-element.3) | copy-start | bytes 1769476
  350.1 19.9 %collective-permute-start.10 = (bf16[1,256,384]{2,1,0:T(8,128)(2,1)}, bf16[1,256,384]{2,1,0:T(8,128)(2,1)}, u32[]{:S(2)}, u32[]{:S(2)}) collective-permute-start(bf16[1,256,384]{2,1,0:T(8,128)(2,1)} %fusion.70), channel_id=1, source_target_pairs={{0,16},{8,24},{16,32},{24,40},{32,48},{40,56},{48,64},{56,72},{64,... | collective-permute-start | bytes 589832 | tf_op jit(solution)/shard_map/ppermute | solution.py:26
  357.0 14.5 %collective-permute-start.9 = (bf16[1,256,384]{2,1,0:T(8,128)(2,1)}, bf16[1,256,384]{2,1,0:T(8,128)(2,1)}, u32[]{:S(2)}, u32[]{:S(2)}) collective-permute-start(bf16[1,256,384]{2,1,0:T(8,128)(2,1)} %fusion.70), channel_id=1, source_target_pairs={{16,0},{24,8},{32,16},{40,24},{48,32},{56,40},{64,48},{72,56},{80,... | collective-permute-start | bytes 589832 | tf_op jit(solution)/shard_map/ppermute | solution.py:26
  364.8 31.0 %collective-permute-start.4 = (bf16[1,256,768]{2,1,0:T(8,128)(2,1)}, bf16[1,256,768]{2,1,0:T(8,128)(2,1)S(1)}, u32[]{:S(2)}, u32[]{:S(2)}) collective-permute-start(bf16[1,256,768]{2,1,0:T(8,128)(2,1)} %fusion.5), channel_id=1, source_target_pairs={{7,0},{0,1},{1,2},{2,3},{3,4},{4,5},{5,6},{6,7},{15,8},{8,9},{9,10... | collective-permute-start | bytes 1179656 | tf_op jit(solution)/shard_map/ppermute | solution.py:32
  368.2 3.3 copy-start.20
  370.0 1.5 copy-start.8
  370.1 1.5 copy-start.16
  371.5 1.9 copy-start.10
  371.5 1.9 copy-start.18
  374.0 11.3 %collective-permute-start.12 = (bf16[1,128,384]{2,1,0:T(8,128)(2,1)S(1)}, bf16[1,128,384]{2,1,0:T(8,128)(2,1)S(1)}, u32[]{:S(2)}, u32[]{:S(2)}) collective-permute-start(bf16[1,128,384]{2,1,0:T(8,128)(2,1)S(1)} %get-tuple-element.15), channel_id=1, source_target_pairs={{0,8},{8,16},{16,24},{24,32},{32,40},{40,48},{48,56},{56,64},{64,7... | collective-permute-start | bytes 294920 | tf_op jit(solution)/shard_map/ppermute | solution.py:17
  383.3 9.8 %copy-start.6 = (bf16[1,1,1,768,384]{4,1,2,0,3:T(2,128)(2,1)S(1)}, bf16[1,1,1,768,384]{4,1,2,0,3:T(2,128)(2,1)}, u32[]{:S(2)}) copy-start(bf16[1,1,1,768,384]{4,1,2,0,3:T(2,128)(2,1)} %copy-done.5) | copy-start | bytes 1769476
  383.3 9.8 %copy-start.14 = (bf16[1,256,768]{2,1,0:T(8,128)(2,1)S(1)}, bf16[1,256,768]{2,1,0:T(8,128)(2,1)}, u32[]{:S(2)}) copy-start(bf16[1,256,768]{2,1,0:T(8,128)(2,1)} %param.6) | copy-start | bytes 1179652
  383.3 9.8 %collective-permute-start.11 = (bf16[1,128,384]{2,1,0:T(8,128)(2,1)S(1)}, bf16[1,128,384]{2,1,0:T(8,128)(2,1)S(1)}, u32[]{:S(2)}, u32[]{:S(2)}) collective-permute-start(bf16[1,128,384]{2,1,0:T(8,128)(2,1)S(1)} %get-tuple-element.14), channel_id=1, source_target_pairs={{8,0},{16,8},{24,16},{32,24},{40,32},{48,40},{56,48},{64,56},{72,6... | collective-permute-start | bytes 294920 | tf_op jit(solution)/shard_map/ppermute | solution.py:18
  393.9 9.4 %collective-permute-start.13 = (bf16[1,256,768]{2,1,0:T(8,128)(2,1)S(1)}, bf16[1,256,768]{2,1,0:T(8,128)(2,1)S(1)}, u32[]{:S(2)}, u32[]{:S(2)}) collective-permute-start(bf16[1,256,768]{2,1,0:T(8,128)(2,1)S(1)} %fusion.28), channel_id=1, source_target_pairs={{1,0},{2,1},{3,2},{4,3},{5,4},{6,5},{7,6},{0,7},{9,8},{10,9},{11,1... | collective-permute-start | bytes 1179656 | tf_op jit(solution)/shard_map/ppermute | solution.py:32
  (5 other events, 6.0 us)
Sparse Core Ops, SparseCore 0:
  11.2 143.1 all-gather.4
  157.7 143.1 all-gather.2
where the time goes:
time: 413 us; the launch traced here: 412 us
  waiting for transfers between devices  287 us (69%)
  starting transfers between devices  57.1 us (14%)
  matrix products  30 us (7%)
  local copies, waits for them, and re-layouts  21.2 us (5%)
  between operations  14.5 us (4%)
    all_gather x1, waiting for transfers between devices, local(): lax.all_gather(conv_weight, 'seq', axis=3, tiled=True)  141 us
    all_gather x1, waiting for transfers between devices, local(): lax.all_gather(proj_weight, 'seq', axis=2, tiled=True)  124 us
    ppermute x6, starting transfers between devices, from_behind(): return lax.ppermute(block, axis, route)  23.6 us
    ppermute x3, starting transfers between devices, padded(): before = lax.ppermute(last, axis, up)  22.2 us
    dot_general x10, matrix products, conv_apply(): jnp.einsum('krc,ch->krh', values, weight, preferred_element_type=jnp.floa...  13.1 us
    slice x1, local copies, waits for them, and re-layouts, run_forward(): middle = conv_apply(activated, conv_part[1])  9.01 us
    dot_general x3, matrix products, run_forward(): jnp.einsum('krh,hc->krc', hidden, proj_part, preferred_element_type=jnp.f...  8.49 us
  transfers between devices with their start and end apart: 16, of which 6 were waited for; matrix products, arithmetic and copies ran while one was open for 12% of the time, Pallas kernels for 0%

commit v1 on v0

--- a/solution.py
+++ b/solution.py
@@ -2,6 +2,7 @@
 import jax.numpy as jnp
 from jax import lax
 from jax.sharding import PartitionSpec as P
+from jax.lax import all_to_all, axis_size
 
 BLOCKS = 2
 FIRST_DILATION = 128
@@ -82,7 +83,9 @@
 def local(fwd_input, bwd_input, bwd_cotangent, conv_weight, proj_weight):
     convolution_complete, proj_full = (
         lax.all_gather(conv_weight, "seq", axis=3, tiled=True),
-        lax.all_gather(proj_weight, "seq", axis=2, tiled=True),
+        jnp.concatenate(
+            all_to_all(jnp.stack(axis_size("seq") * [proj_weight], 0), "seq", 0, 0), axis=2
+        ),
     )
     pieces = [
         (convolution_complete[0, depth_level], proj_full[0, depth_level])

time: 413 us -> 281 us (0.68)
  waiting for transfers between devices: 287 us -> 141 us
  starting transfers between devices: 57.1 us -> 73.2 us
    all_gather x1 -> x0, waiting for transfers between devices: 124 us -> none  [local(): lax.all_gather(proj_weight, 'seq', axis=2, tiled=True)]
    all_gather x1, waiting for transfers between devices: 141 us -> 75 us  [local(): lax.all_gather(conv_weight, 'seq', axis=3, tiled=True)]
    all_to_all x0 -> x1, waiting for transfers between devices: none -> 44.6 us  [local(): all_to_all(jnp.stack(axis_size('seq') * [proj_weight], 0), 'seq', 0, 0)]
    all_to_all x0 -> x1, starting transfers between devices: none -> 17.7 us  [local(): all_to_all(jnp.stack(axis_size('seq') * [proj_weight], 0), 'seq', 0, 0)]
  transfers between devices with their start and end apart: 16 -> 16, of which waited for: 6 -> 6; matrix products, arithmetic and copies ran while one was open for 12% -> 17% of each run, Pallas kernels for 0% -> 0%
where the time goes in v1:
time: 281 us; the launch traced here: 280 us
  waiting for transfers between devices  141 us (50%)
  starting transfers between devices  73.2 us (26%)
  matrix products  30 us (11%)
  local copies, waits for them, and re-layouts  20.8 us (7%)
  between operations  14.5 us (5%)
    all_gather x1, waiting for transfers between devices, local(): lax.all_gather(conv_weight, 'seq', axis=3, tiled=True)  75 us
    all_to_all x1, waiting for transfers between devices, local(): all_to_all(jnp.stack(axis_size('seq') * [proj_weight], 0), 'seq', 0, 0)  44.6 us
    ppermute x6, starting transfers between devices, from_behind(): return lax.ppermute(block, axis, route)  23.6 us
    ppermute x3, starting transfers between devices, padded(): before = lax.ppermute(last, axis, up)  20.7 us
    all_to_all x1, starting transfers between devices, local(): all_to_all(jnp.stack(axis_size('seq') * [proj_weight], 0), 'seq', 0, 0)  17.7 us
    dot_general x10, matrix products, conv_apply(): jnp.einsum('krc,ch->krh', values, weight, preferred_element_type=jnp.floa...  13.1 us
    slice x1, local copies, waits for them, and re-layouts, run_forward(): middle = conv_apply(activated, conv_part[1])  9.01 us
    dot_general x3, matrix products, run_forward(): jnp.einsum('krh,hc->krc', hidden, proj_part, preferred_element_type=jnp.f...  8.48 us
  transfers between devices with their start and end apart: 16, of which 6 were waited for; matrix products, arithmetic and copies ran while one was open for 17% of the time, Pallas kernels for 0%

profile of v1, /device:TPU:103, one launch (start us, length us, event | category | flops | bytes accessed | tf_op | source)
XLA Modules:
  0.0 279.9 jit_solution(12431089959340973314)
XLA Ops:
  7.2 1.5 copy.10
  8.7 2.3 stack.2
  11.1 17.7 %all-to-all-start = ((bf16[64,1,2,6,768]{4,2,3,1,0:T(2,128)(2,1)}), bf16[64,1,2,6,768]{4,2,3,1,0:T(2,128)(2,1)S(1)}, u32[]{:S(2)}, u32[]{:S(2)}) async-start(bf16[64,1,2,6,768]{4,2,3,1,0:T(2,128)(2,1)} %stack.2), calls=%async_computation | async-start | bytes 2359296 | tf_op jit(solution)/shard_map/all_to_all | solution.py:87
  29.9 4.6 %collective-permute-start.5 = (bf16[1,128,768]{2,1,0:T(8,128)(2,1)}, bf16[1,128,768]{2,1,0:T(8,128)(2,1)}, u32[]{:S(2)}, u32[]{:S(2)}) collective-permute-start(bf16[1,128,768]{2,1,0:T(8,128)(2,1)} %get-tuple-element.10), channel_id=1, source_target_pairs={{0,8},{8,16},{16,24},{24,32},{32,40},{40,48},{48,56},{56,64},{64,7... | collective-permute-start | bytes 589832 | tf_op jit(solution)/shard_map/ppermute | solution.py:18
  34.5 1.9 collective-permute-start.6
  37.6 7.2 %collective-permute-start = (bf16[1,128,768]{2,1,0:T(8,128)(2,1)}, bf16[1,128,768]{2,1,0:T(8,128)(2,1)}, u32[]{:S(2)}, u32[]{:S(2)}) collective-permute-start(bf16[1,128,768]{2,1,0:T(8,128)(2,1)} %get-tuple-element.12), channel_id=1, source_target_pairs={{0,8},{8,16},{16,24},{24,32},{32,40},{40,48},{48,56},{56,64},{64,7... | collective-permute-start | bytes 589832 | tf_op jit(solution)/shard_map/ppermute | solution.py:18
  44.8 1.9 collective-permute-start.1
  46.8 44.6 %all-to-all-done = bf16[64,1,2,6,768]{4,2,3,1,0:T(2,128)(2,1)S(1)} async-done(((bf16[64,1,2,6,768]{4,2,3,1,0:T(2,128)(2,1)}), bf16[64,1,2,6,768]{4,2,3,1,0:T(2,128)(2,1)S(1)}, u32[]{:S(2)}, u32[]{:S(2)}) %all-to-all-start) | async-done | bytes 1179680 | tf_op jit(solution)/shard_map/all_to_all | solution.py:87
  91.4 3.0 %fusion.186 = (bf16[1,1,384,768]{3,1,2,0:T(2,128)(2,1)}, bf16[1,1,384,768]{3,1,2,0:T(2,128)(2,1)}) fusion(bf16[1,2,384,768]{3,1,2,0:T(2,128)(2,1)S(1)} %bitcast.233), kind=kLoop, calls=%fused_computation.223 | loop fusion | bytes 2359296 | tf_op jit(solution)/shard_map/slice | solution.py:91
  94.4 75.0 %all-gather.2.cloned.1.call-done = bf16[1,2,3,768,384]{4,1,2,0,3:T(2,128)(2,1)} async-done(((bf16[1,2,3,12,384]{4,1,2,0,3:T(2,128)(2,1)}), bf16[1,2,3,768,384]{4,1,2,0,3:T(2,128)(2,1)}) %all-gather.2.cloned.1.call-update) | async-done | bytes 3538960 | tf_op jit(solution)/shard_map/all_gather | solution.py:85
  169.3 9.0 %fusion.185 = (bf16[1,1,1,768,384]{4,1,2,0,3:T(2,128)(2,1)}, bf16[1,1,1,768,384]{4,1,2,0,3:T(2,128)(2,1)}, bf16[1,1,1,768,384]{4,1,2,0,3:T(2,128)(2,1)S(1)}, bf1...) fusion(bf16[1,2,3,768,384]{4,1,2,0,3:T(2,128)(2,1)} %all-gather, ...), kind=kLoop, calls=%fused_computation.222 | loop fusion | bytes 7077888 | tf_op jit(solution)/shard_map/slice | solution.py:69
  178.4 1.5 fusion.19
  184.0 3.8 %collective-permute-start.7 = (bf16[1,256,768]{2,1,0:T(8,128)(2,1)}, bf16[1,256,768]{2,1,0:T(8,128)(2,1)}, u32[]{:S(2)}, u32[]{:S(2)}) collective-permute-start(bf16[1,256,768]{2,1,0:T(8,128)(2,1)} %get-tuple-element.18), channel_id=1, source_target_pairs={{0,16},{8,24},{16,32},{24,40},{32,48},{40,56},{48,64},{56,72},{64,... | collective-permute-start | bytes 1179656 | tf_op jit(solution)/shard_map/ppermute | solution.py:27
  187.8 3.0 %collective-permute-start.8 = (bf16[1,256,768]{2,1,0:T(8,128)(2,1)}, bf16[1,256,768]{2,1,0:T(8,128)(2,1)}, u32[]{:S(2)}, u32[]{:S(2)}) collective-permute-start(bf16[1,256,768]{2,1,0:T(8,128)(2,1)} %get-tuple-element.18), channel_id=1, source_target_pairs={{16,0},{24,8},{32,16},{40,24},{48,32},{56,40},{64,48},{72,56},{80,... | collective-permute-start | bytes 1179656 | tf_op jit(solution)/shard_map/ppermute | solution.py:27
  190.8 2.0 fusion.15
  192.8 2.0 fusion.16
  194.8 3.5 %fusion.44 = (bf16[1,256,768]{2,1,0:T(8,128)(2,1)}, bf16[1,256,768]{2,1,0:T(8,128)(2,1)}) fusion(bf16[1,1,384,768]{3,1,2,0:T(2,128)(2,1)} %get-tuple-element.9, bf16[1,256,384]{2,1,0:T(8,128)(2,1)} %fusion.16, bf16[1,256,384]{2,1,0:T(8,128)(2,1)} %fusion.15, bf16[1,1,1,768,384]{4,1,2,0,3:T(2,128)(2,1)S(1)} %get-tuple-element.5, bf16[1,256,768]{2,1,0:T(8,128)(2,1)} %param.5), kind=kOutput, calls=%fused_computation.84 | convolution fusion | flops 307789824 | bytes 2752512 | tf_op jit(solution)/shard_map/krh,hc->krc/dot_general | solution.py:78
  198.3 5.9 %collective-permute-start.2 = (bf16[1,256,768]{2,1,0:T(8,128)(2,1)}, bf16[1,256,768]{2,1,0:T(8,128)(2,1)S(1)}, u32[]{:S(2)}, u32[]{:S(2)}) collective-permute-start(bf16[1,256,768]{2,1,0:T(8,128)(2,1)} %get-tuple-element.16), channel_id=1, source_target_pairs={{0,16},{8,24},{16,32},{24,40},{32,48},{40,56},{48,64},{56,72},{64,... | collective-permute-start | bytes 1179656 | tf_op jit(solution)/shard_map/ppermute | solution.py:27
  204.2 2.1 collective-permute-start.3
  206.5 1.9 fusion.21
  208.4 6.2 %collective-permute-done.8 = bf16[1,256,768]{2,1,0:T(8,128)(2,1)} collective-permute-done((bf16[1,256,768]{2,1,0:T(8,128)(2,1)}, bf16[1,256,768]{2,1,0:T(8,128)(2,1)}, u32[]{:S(2)}, u32[]{:S(2)}) %collective-permute-start.8) | collective-permute-done | bytes 393248 | tf_op jit(solution)/shard_map/ppermute | solution.py:27
  218.5 6.9 %collective-permute-start.10 = (bf16[1,256,384]{2,1,0:T(8,128)(2,1)}, bf16[1,256,384]{2,1,0:T(8,128)(2,1)}, u32[]{:S(2)}, u32[]{:S(2)}) collective-permute-start(bf16[1,256,384]{2,1,0:T(8,128)(2,1)} %fusion.75), channel_id=1, source_target_pairs={{0,16},{8,24},{16,32},{24,40},{32,48},{40,56},{48,64},{56,72},{64,... | collective-permute-start | bytes 589832 | tf_op jit(solution)/shard_map/ppermute | solution.py:27
  225.5 1.9 collective-permute-start.9
  229.5 3.5 %fusion.5 = bf16[1,256,768]{2,1,0:T(8,128)(2,1)} fusion(bf16[1,256,768]{2,1,0:T(8,128)(2,1)} %get-tuple-element.17, bf16[1,256,384]{2,1,0:T(8,128)(2,1)} %fusion.18, bf16[1,256,384]{2,1,0:T(8,128)(2,1)} %fusion.17, bf16[1,1,384,768]{3,1,2,0:T(2,128)(2,1)} %get-tuple-element.8, bf16[1,1,1,768,384]{4,1,2,0,3:T(2,128)(2,1)} %get-tuple-element.2), kind=kOutput, calls=%fused_computation.31 | convolution fusion | flops 305823744 | bytes 2359296 | tf_op jit(solution)/shard_map/krh,hc->krc/dot_general | solution.py:78
  233.0 3.4 %collective-permute-start.4 = (bf16[1,256,768]{2,1,0:T(8,128)(2,1)}, bf16[1,256,768]{2,1,0:T(8,128)(2,1)S(1)}, u32[]{:S(2)}, u32[]{:S(2)}) collective-permute-start(bf16[1,256,768]{2,1,0:T(8,128)(2,1)} %fusion.5), channel_id=1, source_target_pairs={{7,0},{0,1},{1,2},{2,3},{3,4},{4,5},{5,6},{6,7},{15,8},{8,9},{9,10... | collective-permute-start | bytes 1179656 | tf_op jit(solution)/shard_map/ppermute | solution.py:33
  236.5 1.8 fusion.143
  239.8 1.9 fusion.32
  242.2 8.8 %collective-permute-start.12 = (bf16[1,128,384]{2,1,0:T(8,128)(2,1)S(1)}, bf16[1,128,384]{2,1,0:T(8,128)(2,1)S(1)}, u32[]{:S(2)}, u32[]{:S(2)}) collective-permute-start(bf16[1,128,384]{2,1,0:T(8,128)(2,1)S(1)} %get-tuple-element.15), channel_id=1, source_target_pairs={{0,8},{8,16},{16,24},{24,32},{32,40},{40,48},{48,56},{56,64},{64,7... | collective-permute-start | bytes 294920 | tf_op jit(solution)/shard_map/ppermute | solution.py:18
  251.5 2.1 collective-permute-start.11
  254.0 7.3 %collective-permute-done.11 = bf16[1,128,384]{2,1,0:T(8,128)(2,1)S(1)} collective-permute-done((bf16[1,128,384]{2,1,0:T(8,128)(2,1)S(1)}, bf16[1,128,384]{2,1,0:T(8,128)(2,1)S(1)}, u32[]{:S(2)}, u32[]{:S(2)}) %collective-permute-start.11) | collective-permute-done | bytes 98336 | tf_op jit(solution)/shard_map/ppermute | solution.py:19
  262.1 1.9 collective-permute-start.13
  264.0 7.5 %collective-permute-done.13 = bf16[1,256,768]{2,1,0:T(8,128)(2,1)S(1)} collective-permute-done((bf16[1,256,768]{2,1,0:T(8,128)(2,1)S(1)}, bf16[1,256,768]{2,1,0:T(8,128)(2,1)S(1)}, u32[]{:S(2)}, u32[]{:S(2)}) %collective-permute-start.13) | collective-permute-done | bytes 393248 | tf_op jit(solution)/shard_map/ppermute | solution.py:33
  (77 shorter events, 17.7 us)
Async XLA Ops:
  7.2 162.2 %all-gather.2.cloned.1.call-start = ((), (), s32[]{:S(2)}) async-start(), calls=%async_computation.1 | async-start | bytes 3594240 | tf_op jit(solution)/shard_map/all_gather | solution.py:85
  11.1 17.7 %copy-start.13 = (bf16[1,256,768]{2,1,0:T(8,128)(2,1)S(1)}, bf16[1,256,768]{2,1,0:T(8,128)(2,1)}, u32[]{:S(2)}) copy-start(bf16[1,256,768]{2,1,0:T(8,128)(2,1)} %param.6) | copy-start | bytes 1179652
  11.1 80.3 %all-to-all-start = ((bf16[64,1,2,6,768]{4,2,3,1,0:T(2,128)(2,1)}), bf16[64,1,2,6,768]{4,2,3,1,0:T(2,128)(2,1)S(1)}, u32[]{:S(2)}, u32[]{:S(2)}) async-start(bf16[64,1,2,6,768]{4,2,3,1,0:T(2,128)(2,1)} %stack.2), calls=%async_computation | async-start | bytes 2359296 | tf_op jit(solution)/shard_map/all_to_all | solution.py:87
  28.7 7.7 %copy-start.12 = (bf16[1,256,768]{2,1,0:T(8,128)(2,1)S(1)}, bf16[1,256,768]{2,1,0:T(8,128)(2,1)}, u32[]{:S(2)}) copy-start(bf16[1,256,768]{2,1,0:T(8,128)(2,1)} %param.5) | copy-start | bytes 1179652
  29.0 5.4 %copy-start.3 = (bf16[1,256,768]{2,1,0:T(8,128)(2,1)}, bf16[1,256,768]{2,1,0:T(8,128)(2,1)S(1)}, u32[]{:S(2)}) copy-start(bf16[1,256,768]{2,1,0:T(8,128)(2,1)S(1)} %fusion.54) | copy-start | bytes 1179652
  29.9 148.5 %collective-permute-start.5 = (bf16[1,128,768]{2,1,0:T(8,128)(2,1)}, bf16[1,128,768]{2,1,0:T(8,128)(2,1)}, u32[]{:S(2)}, u32[]{:S(2)}) collective-permute-start(bf16[1,128,768]{2,1,0:T(8,128)(2,1)} %get-tuple-element.10), channel_id=1, source_target_pairs={{0,8},{8,16},{16,24},{24,32},{32,40},{40,48},{48,56},{56,64},{64,7... | collective-permute-start | bytes 589832 | tf_op jit(solution)/shard_map/ppermute | solution.py:18
  34.5 145.4 %collective-permute-start.6 = (bf16[1,128,768]{2,1,0:T(8,128)(2,1)}, bf16[1,128,768]{2,1,0:T(8,128)(2,1)}, u32[]{:S(2)}, u32[]{:S(2)}) collective-permute-start(bf16[1,128,768]{2,1,0:T(8,128)(2,1)} %get-tuple-element.11), channel_id=1, source_target_pairs={{8,0},{16,8},{24,16},{32,24},{40,32},{48,40},{56,48},{64,56},{72,6... | collective-permute-start | bytes 589832 | tf_op jit(solution)/shard_map/ppermute | solution.py:19
  36.7 57.7 %copy-start.1 = (bf16[1,256,768]{2,1,0:T(8,128)(2,1)}, bf16[1,256,768]{2,1,0:T(8,128)(2,1)S(1)}, u32[]{:S(2)}) copy-start(bf16[1,256,768]{2,1,0:T(8,128)(2,1)S(1)} %fusion.38) | copy-start | bytes 1179652
  37.6 153.2 %collective-permute-start = (bf16[1,128,768]{2,1,0:T(8,128)(2,1)}, bf16[1,128,768]{2,1,0:T(8,128)(2,1)}, u32[]{:S(2)}, u32[]{:S(2)}) collective-permute-start(bf16[1,128,768]{2,1,0:T(8,128)(2,1)} %get-tuple-element.12), channel_id=1, source_target_pairs={{0,8},{8,16},{16,24},{24,32},{32,40},{40,48},{48,56},{56,64},{64,7... | collective-permute-start | bytes 589832 | tf_op jit(solution)/shard_map/ppermute | solution.py:18
  44.8 148.0 %collective-permute-start.1 = (bf16[1,128,768]{2,1,0:T(8,128)(2,1)}, bf16[1,128,768]{2,1,0:T(8,128)(2,1)}, u32[]{:S(2)}, u32[]{:S(2)}) collective-permute-start(bf16[1,128,768]{2,1,0:T(8,128)(2,1)} %get-tuple-element.13), channel_id=1, source_target_pairs={{8,0},{16,8},{24,16},{32,24},{40,32},{48,40},{56,48},{64,56},{72,6... | collective-permute-start | bytes 589832 | tf_op jit(solution)/shard_map/ppermute | solution.py:19
  169.3 9.0 %copy-start.4 = (bf16[1,256,768]{2,1,0:T(8,128)(2,1)S(1)}, bf16[1,256,768]{2,1,0:T(8,128)(2,1)}, u32[]{:S(2)}) copy-start(bf16[1,256,768]{2,1,0:T(8,128)(2,1)} %copy-done.3) | copy-start | bytes 1179652
  178.4 12.5 %copy-start.5 = (bf16[1,1,1,768,384]{4,1,2,0,3:T(2,128)(2,1)}, bf16[1,1,1,768,384]{4,1,2,0,3:T(2,128)(2,1)S(1)}, u32[]{:S(2)}) copy-start(bf16[1,1,1,768,384]{4,1,2,0,3:T(2,128)(2,1)S(1)} %get-tuple-element.6) | copy-start | bytes 1769476
  181.8 2.2 copy-start.18
  182.6 8.3 %copy-start.2 = (bf16[1,256,768]{2,1,0:T(8,128)(2,1)S(1)}, bf16[1,256,768]{2,1,0:T(8,128)(2,1)}, u32[]{:S(2)}) copy-start(bf16[1,256,768]{2,1,0:T(8,128)(2,1)} %copy-done.1) | copy-start | bytes 1179652
  184.0 22.5 %collective-permute-start.7 = (bf16[1,256,768]{2,1,0:T(8,128)(2,1)}, bf16[1,256,768]{2,1,0:T(8,128)(2,1)}, u32[]{:S(2)}, u32[]{:S(2)}) collective-permute-start(bf16[1,256,768]{2,1,0:T(8,128)(2,1)} %get-tuple-element.18), channel_id=1, source_target_pairs={{0,16},{8,24},{16,32},{24,40},{32,48},{40,56},{48,64},{56,72},{64,... | collective-permute-start | bytes 1179656 | tf_op jit(solution)/shard_map/ppermute | solution.py:27
  187.8 26.8 %collective-permute-start.8 = (bf16[1,256,768]{2,1,0:T(8,128)(2,1)}, bf16[1,256,768]{2,1,0:T(8,128)(2,1)}, u32[]{:S(2)}, u32[]{:S(2)}) collective-permute-start(bf16[1,256,768]{2,1,0:T(8,128)(2,1)} %get-tuple-element.18), channel_id=1, source_target_pairs={{16,0},{24,8},{32,16},{40,24},{48,32},{56,40},{64,48},{72,56},{80,... | collective-permute-start | bytes 1179656 | tf_op jit(solution)/shard_map/ppermute | solution.py:27
  198.3 29.1 %collective-permute-start.2 = (bf16[1,256,768]{2,1,0:T(8,128)(2,1)}, bf16[1,256,768]{2,1,0:T(8,128)(2,1)S(1)}, u32[]{:S(2)}, u32[]{:S(2)}) collective-permute-start(bf16[1,256,768]{2,1,0:T(8,128)(2,1)} %get-tuple-element.16), channel_id=1, source_target_pairs={{0,16},{8,24},{16,32},{24,40},{32,48},{40,56},{48,64},{56,72},{64,... | collective-permute-start | bytes 1179656 | tf_op jit(solution)/shard_map/ppermute | solution.py:27
  204.2 24.2 %collective-permute-start.3 = (bf16[1,256,768]{2,1,0:T(8,128)(2,1)}, bf16[1,256,768]{2,1,0:T(8,128)(2,1)S(1)}, u32[]{:S(2)}, u32[]{:S(2)}) collective-permute-start(bf16[1,256,768]{2,1,0:T(8,128)(2,1)} %get-tuple-element.16), channel_id=1, source_target_pairs={{16,0},{24,8},{32,16},{40,24},{48,32},{56,40},{64,48},{72,56},{80,... | collective-permute-start | bytes 1179656 | tf_op jit(solution)/shard_map/ppermute | solution.py:27
  206.5 9.4 %copy-start = (bf16[1,1,1,768,384]{4,1,2,0,3:T(2,128)(2,1)S(1)}, bf16[1,1,1,768,384]{4,1,2,0,3:T(2,128)(2,1)}, u32[]{:S(2)}) copy-start(bf16[1,1,1,768,384]{4,1,2,0,3:T(2,128)(2,1)} %get-tuple-element.2) | copy-start | bytes 1769476
  206.5 9.4 %copy-start.20 = (bf16[1,256,768]{2,1,0:T(8,128)(2,1)S(1)}, bf16[1,256,768]{2,1,0:T(8,128)(2,1)}, u32[]{:S(2)}) copy-start(bf16[1,256,768]{2,1,0:T(8,128)(2,1)} %get-tuple-element.19) | copy-start | bytes 1179652
  217.3 10.1 %copy-start.7 = (bf16[1,1,1,768,384]{4,1,2,0,3:T(2,128)(2,1)S(1)}, bf16[1,1,1,768,384]{4,1,2,0,3:T(2,128)(2,1)}, u32[]{:S(2)}) copy-start(bf16[1,1,1,768,384]{4,1,2,0,3:T(2,128)(2,1)} %get-tuple-element.3) | copy-start | bytes 1769476
  218.5 19.8 %collective-permute-start.10 = (bf16[1,256,384]{2,1,0:T(8,128)(2,1)}, bf16[1,256,384]{2,1,0:T(8,128)(2,1)}, u32[]{:S(2)}, u32[]{:S(2)}) collective-permute-start(bf16[1,256,384]{2,1,0:T(8,128)(2,1)} %fusion.75), channel_id=1, source_target_pairs={{0,16},{8,24},{16,32},{24,40},{32,48},{40,56},{48,64},{56,72},{64,... | collective-permute-start | bytes 589832 | tf_op jit(solution)/shard_map/ppermute | solution.py:27
  225.5 14.3 %collective-permute-start.9 = (bf16[1,256,384]{2,1,0:T(8,128)(2,1)}, bf16[1,256,384]{2,1,0:T(8,128)(2,1)}, u32[]{:S(2)}, u32[]{:S(2)}) collective-permute-start(bf16[1,256,384]{2,1,0:T(8,128)(2,1)} %fusion.75), channel_id=1, source_target_pairs={{16,0},{24,8},{32,16},{40,24},{48,32},{56,40},{64,48},{72,56},{80,... | collective-permute-start | bytes 589832 | tf_op jit(solution)/shard_map/ppermute | solution.py:27
  233.0 31.0 %collective-permute-start.4 = (bf16[1,256,768]{2,1,0:T(8,128)(2,1)}, bf16[1,256,768]{2,1,0:T(8,128)(2,1)S(1)}, u32[]{:S(2)}, u32[]{:S(2)}) collective-permute-start(bf16[1,256,768]{2,1,0:T(8,128)(2,1)} %fusion.5), channel_id=1, source_target_pairs={{7,0},{0,1},{1,2},{2,3},{3,4},{4,5},{5,6},{6,7},{15,8},{8,9},{9,10... | collective-permute-start | bytes 1179656 | tf_op jit(solution)/shard_map/ppermute | solution.py:33
  236.4 3.3 %copy-start.21 = (bf16[1,256,768]{2,1,0:T(8,128)(2,1)S(1)}, bf16[1,256,768]{2,1,0:T(8,128)(2,1)}, u32[]{:S(2)}) copy-start(bf16[1,256,768]{2,1,0:T(8,128)(2,1)} %get-tuple-element.19) | copy-start | bytes 1179652
  239.7 1.9 copy-start.10
  239.8 1.9 copy-start.19
  242.2 11.3 %collective-permute-start.12 = (bf16[1,128,384]{2,1,0:T(8,128)(2,1)S(1)}, bf16[1,128,384]{2,1,0:T(8,128)(2,1)S(1)}, u32[]{:S(2)}, u32[]{:S(2)}) collective-permute-start(bf16[1,128,384]{2,1,0:T(8,128)(2,1)S(1)} %get-tuple-element.15), channel_id=1, source_target_pairs={{0,8},{8,16},{16,24},{24,32},{32,40},{40,48},{48,56},{56,64},{64,7... | collective-permute-start | bytes 294920 | tf_op jit(solution)/shard_map/ppermute | solution.py:18
  251.5 9.8 %copy-start.6 = (bf16[1,1,1,768,384]{4,1,2,0,3:T(2,128)(2,1)S(1)}, bf16[1,1,1,768,384]{4,1,2,0,3:T(2,128)(2,1)}, u32[]{:S(2)}) copy-start(bf16[1,1,1,768,384]{4,1,2,0,3:T(2,128)(2,1)} %copy-done.5) | copy-start | bytes 1769476
  251.5 9.8 %copy-start.15 = (bf16[1,256,768]{2,1,0:T(8,128)(2,1)S(1)}, bf16[1,256,768]{2,1,0:T(8,128)(2,1)}, u32[]{:S(2)}) copy-start(bf16[1,256,768]{2,1,0:T(8,128)(2,1)} %param.6) | copy-start | bytes 1179652
  251.5 9.8 %collective-permute-start.11 = (bf16[1,128,384]{2,1,0:T(8,128)(2,1)S(1)}, bf16[1,128,384]{2,1,0:T(8,128)(2,1)S(1)}, u32[]{:S(2)}, u32[]{:S(2)}) collective-permute-start(bf16[1,128,384]{2,1,0:T(8,128)(2,1)S(1)} %get-tuple-element.14), channel_id=1, source_target_pairs={{8,0},{16,8},{24,16},{32,24},{40,32},{48,40},{56,48},{64,56},{72,6... | collective-permute-start | bytes 294920 | tf_op jit(solution)/shard_map/ppermute | solution.py:19
  262.1 9.4 %collective-permute-start.13 = (bf16[1,256,768]{2,1,0:T(8,128)(2,1)S(1)}, bf16[1,256,768]{2,1,0:T(8,128)(2,1)S(1)}, u32[]{:S(2)}, u32[]{:S(2)}) collective-permute-start(bf16[1,256,768]{2,1,0:T(8,128)(2,1)S(1)} %fusion.28), channel_id=1, source_target_pairs={{1,0},{2,1},{3,2},{4,3},{5,4},{6,5},{7,6},{0,7},{9,8},{10,9},{11,1... | collective-permute-start | bytes 1179656 | tf_op jit(solution)/shard_map/ppermute | solution.py:33
  (6 other events, 8.3 us)
Sparse Core Ops, SparseCore 0:
  11.3 158.0 all-gather.1
